TPU v7x, 32 devices: a whole 2x2x4 slice. The times are simulated.
32 devices in a mesh: grp: 2 (over y), row: 4 (over z), head: 2 (over x), rep: 2 (over core).
Axes of the slice: x: 2, y: 2, z: 4, core: 2. Of those that a mesh axis runs over, the one named last changes fastest.
Arguments:
- queries: float32 [2048, 8192], P(('grp', 'row', 'rep'), 'head'), parts along dimension 0
- key_max: float32 [4096, 1024], P(('grp', 'row', 'rep'), 'head'), parts along dimension 0
- key_min: float32 [4096, 1024], P(('grp', 'row', 'rep'), 'head'), parts along dimension 0, as said below
- limits: int32 [2048], P(('grp', 'row', 'rep')), parts along dimension 0, may hold values from 0 to 2047, as said below
Outputs:
- page_mass: float32 [2048, 2048], P(('grp', 'row', 'rep'), 'head'), parts along dimension 0
There are 2 independent parts, one for each index of `grp`. A program takes and returns all parts, laid end to end along the dimension named above; each array names one. Nothing has to cross between parts.
Inputs may be any that keep to these rules, and one draw needn't show every extreme that they name: key_min <= key_max in every entry. Rows of the i-th aligned block of 128 rows have limits within the i-th block of 256 pages, not falling within a block; the first block's first row has the first page and the last block's last row the last page.
All inputs are finite; a program needn't handle non-finite values.
Results may differ from a plain program's by a relative error of at most 0.00013.
Values sent between devices are 32-bit elements; how exact they have to be, the bound alone decides.
No kernel may reach another device: no remote copies, remote signals or barrier semaphores. Data moves between devices by JAX's collectives and lax.ppermute only.
A program may use at most 64 MiB of HBM per device.

v0:
```python
import math
import jax
import jax.numpy as jnp
from jax import lax
from jax.sharding import PartitionSpec as P

DH = 128


def per_device(queries, key_max, key_min, limits):
    head_count = queries.shape[1] // DH
    kv_count = key_max.shape[1] // DH
    group_size = head_count // kv_count
    score_scale = 1.0 / math.sqrt(DH)
    bounds = jnp.stack((key_max, key_min))
    query_rows, row_limits = (queries, limits)
    gathered = lax.all_gather(bounds, ("row", "rep"), axis=1, tiled=True)
    page_ids = jnp.arange(gathered.shape[1], dtype=jnp.int32)
    row_count = query_rows.shape[0]
    page_count = gathered.shape[1]
    head_rows = query_rows.reshape(row_count, head_count, DH).transpose(1, 0, 2)
    positive = jnp.maximum(head_rows, 0.0)
    negative = jnp.minimum(head_rows, 0.0)
    sheets = gathered.reshape(2, page_count, kv_count, DH).transpose(2, 0, 1, 3)
    visible = page_ids[None, :] <= row_limits[:, None]

    def head_scores(head_index, kv_index):
        upper_part = jnp.dot(
            positive[head_index], sheets[kv_index, 0].T, precision=lax.Precision.HIGHEST
        )
        return upper_part + jnp.dot(
            negative[head_index], sheets[kv_index, 1].T, precision=lax.Precision.HIGHEST
        )

    def head_step(accumulated, head_index):
        raw_scores = head_scores(head_index, head_index // group_size)
        masked = jnp.where(visible, raw_scores * score_scale, -1e30)
        row_top = jnp.max(masked, axis=1, keepdims=True)
        weights = jnp.exp(masked - row_top)
        row_total = jnp.sum(weights, axis=1, keepdims=True)
        return (accumulated + weights / row_total, None)

    start = jnp.zeros((row_count, page_count), jnp.float32)
    accumulated, unused = lax.scan(head_step, start, jnp.arange(head_count, dtype=jnp.int32))
    return lax.psum_scatter(accumulated, "head", scatter_dimension=1, tiled=True)


def solution(mesh):
    placed = (
        P(("grp", "row", "rep"), "head"),
        P(("grp", "row", "rep"), "head"),
        P(("grp", "row", "rep"), "head"),
        P(("grp", "row", "rep")),
    )
    return jax.shard_map(
        per_device,
        mesh=mesh,
        in_specs=placed,
        out_specs=P(("grp", "row", "rep"), "head"),
        check_vma=False,
    )
```

profile of v0, /device:TPU:0, one launch (start us, length us, event | category | flops | bytes accessed | tf_op | source)
XLA Modules:
  0.0 448.6 jit_solution(9973003947528456110)
XLA Ops:
  14.3 80.7 %all-gather.2.cloned.1.call-done = f32[2,2048,512]{1,2,0:T(8,128)} async-done(((f32[2,256,512]{1,2,0:T(8,128)}), f32[2,2048,512]{1,2,0:T(8,128)}) %all-gather.2.cloned.1.call-update) | async-done | bytes 8388624 | tf_op jit(solution)/shard_map/all_gather | solution.py:17
  95.0 8.7 %copy.10 = f32[4,2,2048,128]{3,2,1,0:T(8,128)} copy(f32[4,2,2048,128]{2,3,0,1:T(8,128)} %bitcast.40) | data formatting | bytes 16777216
  103.8 318.0 %while.13 = (s32[]{:T(128)}, f32[128,2048]{1,0:T(8,128)S(1)}, s32[32]{0:T(128)S(1)}, f32[32,128,128]{1,2,0:T(8,128)}, f32[4,2,2048,128]{3,2,1,0:T(8,128)}, /*ind...) while((s32[]{:T(128)}, f32[128,2048]{1,0:T(8,128)S(1)}, ...), condition=%wide.region_3.4_spmd.clone, body=%wide.region_0.3_spmd.clone.sunk | while | flops 808189696 | bytes 9571716 | solution.py:44
  110.4 2.6 fusion.26
  120.4 2.6 fusion.26
  128.0 2.3 fusion.25
  130.3 2.6 fusion.26
  140.3 2.6 fusion.26
  150.2 2.6 fusion.26
  160.1 2.6 fusion.26
  170.1 2.6 fusion.26
  177.7 2.3 fusion.25
  180.0 2.6 fusion.26
  189.9 2.6 fusion.26
  197.5 2.3 fusion.25
  199.9 2.6 fusion.26
  207.5 2.3 fusion.25
  209.8 2.6 fusion.26
  219.7 2.6 fusion.26
  227.4 2.3 fusion.25
  229.7 2.6 fusion.26
  239.6 2.6 fusion.26
  249.6 2.6 fusion.26
  257.2 2.3 fusion.25
  259.5 2.6 fusion.26
  269.4 2.6 fusion.26
  277.0 2.3 fusion.25
  279.4 2.6 fusion.26
  289.3 2.6 fusion.26
  299.2 2.6 fusion.26
  306.8 2.3 fusion.25
  309.2 2.6 fusion.26
  319.1 2.6 fusion.26
  326.7 2.3 fusion.25
  329.1 2.6 fusion.26
  339.0 2.6 fusion.26
  348.9 2.6 fusion.26
  356.5 2.3 fusion.25
  358.9 2.6 fusion.26
  368.8 2.6 fusion.26
  376.4 2.3 fusion.25
  378.7 2.6 fusion.26
  386.3 2.3 fusion.25
  388.7 2.6 fusion.26
  398.6 2.6 fusion.26
  408.5 2.6 fusion.26
  418.5 2.6 fusion.26
  422.7 19.0 %reduce-scatter.2.cloned.1.call-done = f32[128,1024]{1,0:T(8,128)} async-done(((f32[128,2048]{1,0:T(8,128)}), f32[128,1024]{1,0:T(8,128)}) %reduce-scatter.2.cloned.1.call-update) | async-done | bytes 524304 | tf_op jit(solution)/shard_map/reduce_scatter | solution.py:45
  (131 shorter events, 95.5 us)
Async XLA Ops:
  6.5 88.5 %all-gather.2.cloned.1.call-start = ((), (), s32[]{:S(2)}) async-start(), calls=%async_computation.1 | async-start | bytes 9437184 | tf_op jit(solution)/shard_map/all_gather | solution.py:17
  10.1 431.6 %reduce-scatter.2.cloned.1.call-start = ((), (), s32[]{:S(2)}) async-start(), calls=%async_computation.2 | async-start | bytes 1572864 | tf_op jit(solution)/shard_map/reduce_scatter | solution.py:45
  95.0 8.8 %copy-start.1 = (s32[128]{0:T(128)S(1)}, s32[128]{0:T(128)}, u32[]{:S(2)}) copy-start(s32[128]{0:T(128)} %param.9) | copy-start | bytes 1540
  421.7 1.0 copy-start
Sparse Core Ops, SparseCore 0:
  10.2 84.7 all-gather.1
  422.9 18.8 reduce-scatter.1
where the time goes:
time: 452 us; the launch traced here: 449 us
  matrix products  157 us (35%)
  loops' own time  121 us (27%)
  waiting for transfers between devices  99.8 us (22%)
  local copies, waits for them, and re-layouts  33.2 us (7%)
  other arithmetic  24.4 us (5%)
  between operations  13.4 us (3%)
    another operation x1, loops' own time, per_device(): lax.scan(head_step, start, jnp.arange(head_count, dtype=jnp.int32))  121 us
    dot_general x32, matrix products, head_scores(): jnp.dot(negative[head_index], sheets[kv_index, 1].T, precision=lax.Precis...  82.2 us
    all_gather x1, waiting for transfers between devices, per_device(): gathered = lax.all_gather(bounds, ('row', 'rep'), axis=1, tiled=True)  80.7 us
    dot_general x32, matrix products, head_scores(): jnp.dot(positive[head_index], sheets[kv_index, 0].T, precision=lax.Precis...  74.5 us
    dynamic_slice x32, local copies, waits for them, and re-layouts, per_device(): lax.scan(head_step, start, jnp.arange(head_count, dtype=jnp.int32))  19.1 us
    reduce_scatter x1, waiting for transfers between devices, per_device(): lax.psum_scatter(accumulated, 'head', scatter_dimension=1, tiled=True)  19 us
    unnamed x8, local copies, waits for them, and re-layouts  14.1 us
    add x32, other arithmetic, head_step(): return (accumulated + weights / row_total, None)  11.5 us
  transfers between devices with their start and end apart: 2, of which 2 were waited for; matrix products, arithmetic and copies ran while one was open for 1% of the time, Pallas kernels for 0%

commit v1 on v0

--- a/solution.py
+++ b/solution.py
@@ -7,6 +7,24 @@
 DH = 128
 
 
+def laid_out(blocks, dim):
+    blocks = jnp.moveaxis(blocks, 0, dim)
+    shape = blocks.shape
+    return blocks.reshape(*shape[:dim], shape[dim] * shape[dim + 1], *shape[dim + 2 :])
+
+
+def doubled(x, axis):
+    count = lax.axis_size(axis)
+    blocks = x[None]
+    for level in range(count.bit_length() - 1):
+        stride = 1 << level
+        other = lax.ppermute(blocks, axis, [(i, i ^ stride) for i in range(count)])
+        both = jnp.stack([blocks, other])
+        upper = lax.axis_index(axis) >> level & 1
+        blocks = jnp.where(upper == 0, both, both[::-1]).reshape(-1, *x.shape)
+    return blocks
+
+
 def per_device(queries, key_max, key_min, limits):
     head_count = queries.shape[1] // DH
     kv_count = key_max.shape[1] // DH
@@ -14,7 +32,7 @@
     score_scale = 1.0 / math.sqrt(DH)
     bounds = jnp.stack((key_max, key_min))
     query_rows, row_limits = (queries, limits)
-    gathered = lax.all_gather(bounds, ("row", "rep"), axis=1, tiled=True)
+    gathered = laid_out(doubled(bounds, ("row", "rep")), 1)
     page_ids = jnp.arange(gathered.shape[1], dtype=jnp.int32)
     row_count = query_rows.shape[0]
     page_count = gathered.shape[1]

time: 452 us -> 650 us (1.44)
  waiting for transfers between devices: 99.8 us -> 246 us
  local copies, waits for them, and re-layouts: 33.2 us -> 52.1 us
  other arithmetic: 24.4 us -> 40.1 us
  loops' own time: 121 us -> 132 us
    ppermute x0 -> x3, waiting for transfers between devices: none -> 225 us  [doubled(): other = lax.ppermute(blocks, axis, [(i, i ^ stride) for i in range(count)])]
    all_gather x1 -> x0, waiting for transfers between devices: 80.7 us -> none  [per_device(): gathered = lax.all_gather(bounds, ('row', 'rep'), axis=1, tiled=True)]
    another operation x1, loops' own time: 121 us -> 132 us  [per_device(): lax.scan(head_step, start, jnp.arange(head_count, dtype=jnp.int32))]
    reshape x0 -> x1, local copies, waits for them, and re-layouts: none -> 10.4 us  [doubled(): blocks = jnp.where(upper == 0, both, both[::-1]).reshape(-1, *x.shape)]
    another operation x0 -> x1, local copies, waits for them, and re-layouts: none -> 9.25 us  [per_device(): sheets = gathered.reshape(2, page_count, kv_count, DH).transpose(2, 0, 1, 3)]
    another operation x1 -> x5, other arithmetic: 1.04 us -> 10.2 us  [doubled(): both = jnp.stack([blocks, other])]
    select_n x0 -> x2, other arithmetic: none -> 7.02 us  [doubled(): blocks = jnp.where(upper == 0, both, both[::-1]).reshape(-1, *x.shape)]
    unnamed x8 -> x6, local copies, waits for them, and re-layouts: 14.1 us -> 11.6 us
  transfers between devices with their start and end apart: 2 -> 4, of which waited for: 2 -> 4; matrix products, arithmetic and copies ran while one was open for 1% -> 1% of each run, Pallas kernels for 0% -> 0%
where the time goes in v1:
time: 650 us; the launch traced here: 646 us
  waiting for transfers between devices  246 us (38%)
  matrix products  156 us (24%)
  loops' own time  132 us (20%)
  local copies, waits for them, and re-layouts  52.1 us (8%)
  other arithmetic  40.1 us (6%)
  between operations  13.4 us (2%)
    ppermute x3, waiting for transfers between devices, doubled(): other = lax.ppermute(blocks, axis, [(i, i ^ stride) for i in range(count)])  225 us
    another operation x1, loops' own time, per_device(): lax.scan(head_step, start, jnp.arange(head_count, dtype=jnp.int32))  132 us
    dot_general x32, matrix products, head_scores(): jnp.dot(negative[head_index], sheets[kv_index, 1].T, precision=lax.Precis...  81.8 us
    dot_general x32, matrix products, head_scores(): jnp.dot(positive[head_index], sheets[kv_index, 0].T, precision=lax.Precis...  74.5 us
    reduce_scatter x1, waiting for transfers between devices, per_device(): lax.psum_scatter(accumulated, 'head', scatter_dimension=1, tiled=True)  21.5 us
    dynamic_slice x32, local copies, waits for them, and re-layouts, per_device(): lax.scan(head_step, start, jnp.arange(head_count, dtype=jnp.int32))  20.9 us
  transfers between devices with their start and end apart: 4, of which 4 were waited for; matrix products, arithmetic and copies ran while one was open for 1% of the time, Pallas kernels for 0%

profile of v1, /device:TPU:0, one launch (start us, length us, event | category | flops | bytes accessed | tf_op | source)
XLA Modules:
  0.0 646.1 jit_solution(12340322790047109485)
XLA Ops:
  12.8 2.9 collective-permute-start.1
  15.8 46.2 %collective-permute-done.1 = f32[2,2,256,512]{3,2,1,0:T(8,128)} collective-permute-done((f32[2,2,256,512]{3,2,1,0:T(8,128)}, f32[2,2,256,512]{3,2,1,0:T(8,128)}, u32[]{:S(2)}, u32[]{:S(2)}) %collective-permute-start.1) | collective-permute-done | bytes 2097184 | tf_op jit(solution)/shard_map/ppermute | solution.py:21
  64.3 2.7 reverse_select_fusion.1
  67.0 2.8 collective-permute-start.2
  73.9 176.3 %collective-permute-done.2 = f32[4,2,256,512]{3,2,1,0:T(8,128)} collective-permute-done((f32[4,2,256,512]{3,2,1,0:T(8,128)}, f32[4,2,256,512]{3,2,1,0:T(8,128)}, u32[]{:S(2)}, u32[]{:S(2)}) %collective-permute-start.2) | collective-permute-done | bytes 4194336 | tf_op jit(solution)/shard_map/ppermute | solution.py:21
  250.2 4.5 pad_maximum_fusion
  254.7 4.3 reverse_select_fusion
  259.0 10.4 %copy.11 = f32[8,2,256,512]{2,0,3,1:T(8,128)} copy(f32[8,2,256,512]{3,2,1,0:T(8,128)} %bitcast.57) | data formatting | bytes 16777216 | tf_op jit(solution)/shard_map/reshape | solution.py:24
  269.4 9.2 %reshape_reshape.3 = f32[2,2048,4,128]{1,3,2,0:T(8,128)} reshape(f32[2,8,256,512]{2,1,3,0:T(8,128)} %bitcast.58) | data formatting | bytes 16777216 | tf_op jit(solution)/shard_map/reshape;reshape | solution.py:42
  278.7 8.8 %copy.9 = f32[4,2,2048,128]{3,2,1,0:T(8,128)} copy(f32[4,2,2048,128]{2,3,0,1:T(8,128)} %bitcast.59) | data formatting | bytes 16777216
  287.4 329.4 %while.13 = (s32[]{:T(128)}, f32[128,2048]{1,0:T(8,128)S(1)}, s32[32]{0:T(128)S(1)}, f32[32,128,128]{1,2,0:T(8,128)}, f32[4,2,2048,128]{3,2,1,0:T(8,128)}, /*ind...) while((s32[]{:T(128)}, f32[128,2048]{1,0:T(8,128)S(1)}, ...), condition=%wide.region_3.4_spmd.clone, body=%wide.region_0.3_spmd.clone.sunk | while | flops 808189696 | bytes 9571708 | solution.py:62
  294.5 2.6 fusion.30
  304.8 2.6 fusion.30
  312.7 2.3 fusion.29
  315.1 2.6 fusion.30
  325.4 2.6 fusion.30
  335.7 2.6 fusion.30
  346.0 2.6 fusion.30
  353.9 2.3 fusion.29
  356.2 2.6 fusion.30
  366.5 2.6 fusion.30
  374.5 2.3 fusion.29
  376.8 2.6 fusion.30
  387.1 2.6 fusion.30
  397.4 2.6 fusion.30
  407.7 2.6 fusion.30
  415.7 2.3 fusion.29
  418.0 2.6 fusion.30
  428.3 2.6 fusion.30
  438.6 2.6 fusion.30
  448.9 2.6 fusion.30
  459.2 2.6 fusion.30
  469.5 2.6 fusion.30
  479.8 2.6 fusion.30
  490.1 2.6 fusion.30
  500.4 2.6 fusion.30
  510.7 2.6 fusion.30
  521.0 2.6 fusion.30
  531.3 2.6 fusion.30
  541.6 2.6 fusion.30
  551.8 2.6 fusion.30
  562.1 2.6 fusion.30
  572.4 2.6 fusion.30
  582.7 2.6 fusion.30
  593.0 2.6 fusion.30
  603.3 2.6 fusion.30
  613.6 2.6 fusion.30
  617.8 21.5 %reduce-scatter.2.cloned.1.call-done = f32[128,1024]{1,0:T(8,128)} async-done(((f32[128,2048]{1,0:T(8,128)}), f32[128,1024]{1,0:T(8,128)}) %reduce-scatter.2.cloned.1.call-update) | async-done | bytes 524304 | tf_op jit(solution)/shard_map/reduce_scatter | solution.py:63
  (140 shorter events, 120.3 us)
Async XLA Ops:
  6.5 632.7 %reduce-scatter.2.cloned.1.call-start = ((), (), s32[]{:S(2)}) async-start(), calls=%async_computation.1 | async-start | bytes 1572864 | tf_op jit(solution)/shard_map/reduce_scatter | solution.py:63
  8.0 2.8 collective-permute-start
  12.8 49.2 %collective-permute-start.1 = (f32[2,2,256,512]{3,2,1,0:T(8,128)}, f32[2,2,256,512]{3,2,1,0:T(8,128)}, u32[]{:S(2)}, u32[]{:S(2)}) collective-permute-start(f32[2,2,256,512]{3,2,1,0:T(8,128)} %get-tuple-element.149), channel_id=1, source_target_pairs={{0,4},{1,5},{4,0},{5,1},{8,12},{9,13},{12,8},{13,9},{2,6},{3,7},{6... | collective-permute-start | bytes 6291464 | tf_op jit(solution)/shard_map/ppermute | solution.py:21
  67.0 183.2 %collective-permute-start.2 = (f32[4,2,256,512]{3,2,1,0:T(8,128)}, f32[4,2,256,512]{3,2,1,0:T(8,128)}, u32[]{:S(2)}, u32[]{:S(2)}) collective-permute-start(f32[4,2,256,512]{3,2,1,0:T(8,128)} %bitcast.11), channel_id=1, source_target_pairs={{0,8},{1,9},{4,12},{5,13},{8,0},{9,1},{12,4},{13,5},{2,10},{3,11},... | collective-permute-start | bytes 12582920 | tf_op jit(solution)/shard_map/ppermute | solution.py:21
  278.6 8.8 %copy-start.1 = (s32[128]{0:T(128)S(1)}, s32[128]{0:T(128)}, u32[]{:S(2)}) copy-start(s32[128]{0:T(128)} %param.9) | copy-start | bytes 1540
  616.8 1.0 copy-start
Sparse Core Ops, SparseCore 0:
  617.9 21.2 reduce-scatter.1
